TPU v7x, 128 devices: a whole 4x4x4 slice. The times are simulated.
128 devices in a mesh: grp: 2 (over core), fsdp: 64 (over x, y, z).
Axes of the slice: x: 4, y: 4, z: 4, core: 2. Of those that a mesh axis runs over, the one named last changes fastest.
Arguments:
- item_states: bfloat16 [512, 256, 2048], P(('grp', 'fsdp')), may hold values from -6 to 6
- w_query: bfloat16 [2048, 2048], P('fsdp'), may hold values from -0.125 to 0.125
- w_key: bfloat16 [2048, 256], P('fsdp'), may hold values from -0.125 to 0.125
- w_value: bfloat16 [2048, 256], P('fsdp'), may hold values from -0.125 to 0.125
- item_gain: float32 [2048], replicated, may hold values from 0.25 to 1.75
- w_adapt: bfloat16 [2048, 4096], P('fsdp'), may hold values from -0.125 to 0.125
- user_gain: float32 [4096], replicated, may hold values from 0.25 to 1.75
- user_query: bfloat16 [4096, 128], P('fsdp'), may hold values from -0.5 to 0.5
- hist_owner: int32 [128, 128, 1], P(('grp', 'fsdp')), may hold values from 0 to 127; in each aligned block of 128 rows (0 to 127, 128 to 255, ..., all dimensions but the last counted through in order) at most 2 rows name the same one
- history_position_index: int32 [128, 128], P(('grp', 'fsdp')), may hold values from 0 to 3
- cotangent: bfloat16 [128, 128, 4096], P(('grp', 'fsdp')), may hold values from -6 to 6
Outputs:
- item_embed: bfloat16 [512, 2048], P(('grp', 'fsdp'))
- user_attention_output: bfloat16 [128, 128, 4096], P(('grp', 'fsdp'))
- item_grad: float32 [512, 2048], P(('grp', 'fsdp'))
Inputs may be any that keep to these rules, and one draw needn't show every extreme that they name: `hist_owner`: within one history no device is named by more than 2 positions, and some device is named by exactly 2 positions.
All inputs are finite; a program needn't handle non-finite values.
Results may differ from a plain program's by a relative error of at most 0.011.
Values may be sent and summed in bfloat16 or wider, within the bound.
No kernel may reach another device: no remote copies, remote signals or barrier semaphores. Data moves between devices by JAX's collectives and lax.ppermute only.
A program may use at most 128 MiB of HBM per device.

v0:
```python
import jax
import jax.numpy as jnp
from jax import lax
from jax.sharding import PartitionSpec as P

DI = 2048
IHEADS = 32
IHD = 64
IKV = 4
UHEADS = 32
UHD = 128
ILEN = 256


def stored(values):
    return lax.optimization_barrier(values.astype(jnp.bfloat16))


def rms_scale(values, gain):
    mean_sq = jnp.mean(values * values, axis=-1, keepdims=True)
    return values * lax.rsqrt(mean_sq + 1e-05) * gain


def item_pool(states, key_rows, value_rows, query_rows, item_gain):
    count = states.shape[0]
    group = IHEADS // IKV
    query_heads = query_rows.reshape(count, IKV, group, IHD).astype(jnp.float32)
    key_heads = key_rows.reshape(count, ILEN, IKV, IHD).astype(jnp.float32)
    value_heads = value_rows.reshape(count, ILEN, IKV, IHD).astype(jnp.float32)
    scores = jnp.einsum("igrd,itgd->igrt", query_heads, key_heads) * IHD ** (-0.5)
    weights = stored(jax.nn.softmax(scores, axis=-1)).astype(jnp.float32)
    mixed = jnp.einsum("igrt,itgd->igrd", weights, value_heads).reshape(count, IHEADS * IHD)
    last_row = states[:, ILEN - 1, :].astype(jnp.float32)
    return rms_scale(last_row + mixed, item_gain).astype(jnp.bfloat16)


def user_layer(hidden, user_gain, user_query):
    length_total = hidden.shape[0]
    normed = stored(rms_scale(hidden.astype(jnp.float32), user_gain)).astype(jnp.float32)
    heads = normed.reshape(length_total, UHEADS, UHD)
    query_map = user_query.reshape(UHEADS, UHD, UHD).astype(jnp.float32)
    queries = stored(jnp.einsum("thd,hde->the", heads, query_map)).astype(jnp.float32)
    scores = jnp.einsum("the,she->hts", queries, heads) * UHD ** (-0.5)
    target = jnp.arange(length_total, dtype=jnp.int32)
    causal = target[None, :, None] >= target[None, None, :]
    scores = jnp.where(causal, scores, -1e30)
    weights = stored(jax.nn.softmax(scores, axis=-1)).astype(jnp.float32)
    mixed = jnp.einsum("hts,shd->thd", weights, heads).reshape(length_total, UHEADS * UHD)
    return (hidden.astype(jnp.float32) + mixed).astype(jnp.bfloat16)


def serve_rows(requests, lookup_matrix):
    chosen_items = (
        requests[..., None] == jnp.arange(lookup_matrix.shape[0], dtype=jnp.int32)
    ).astype(lookup_matrix.dtype)
    return jnp.einsum(
        "ltj,jy->lty", chosen_items, lookup_matrix, preferred_element_type=jnp.float32
    ).astype(lookup_matrix.dtype)


def per_device(
    item_states,
    w_query,
    w_key,
    w_value,
    item_gain,
    w_adapt,
    user_gain,
    user_query,
    hist_owner,
    history_position_index,
    cotangent,
):
    groups = lax.axis_size("grp")
    shards = lax.axis_size("fsdp")
    devices = groups * shards
    count = item_states.shape[0]
    flat = item_states.reshape(count * ILEN, DI)
    last_row = item_states[:, ILEN - 1, :]
    columns = flat
    key_sum = jnp.dot(
        columns,
        lax.all_gather(w_key, "fsdp", axis=0, tiled=True),
        preferred_element_type=jnp.float32,
    )
    summed_value = jnp.dot(
        columns,
        lax.all_gather(w_value, "fsdp", axis=0, tiled=True),
        preferred_element_type=jnp.float32,
    )
    columns = last_row
    query_sum = jnp.dot(
        columns,
        lax.all_gather(w_query, "fsdp", axis=0, tiled=True),
        preferred_element_type=jnp.float32,
    )
    adapter, query_map = (
        lax.all_gather(w_adapt, "fsdp", axis=0, tiled=True),
        lax.all_gather(user_query, "fsdp", axis=0, tiled=True),
    )
    item_embed = item_pool(
        item_states, stored(key_sum), stored(summed_value), stored(query_sum), item_gain
    )
    length_total = history_position_index.shape[1]
    cap_slots = max(2, 2 * length_total // devices)
    owner_users = hist_owner[0, :, 0]
    owner_hot = (owner_users[:, None] == jnp.arange(devices, dtype=jnp.int32)[None, :]).astype(
        jnp.int32
    )
    earlier = jnp.cumsum(owner_hot, axis=0) - owner_hot
    rank_in = jnp.sum(owner_hot * earlier, axis=1)
    position = owner_users * cap_slots + rank_in
    request = (
        jnp.full((devices * cap_slots,), count, jnp.int32)
        .at[position]
        .set(history_position_index[0])
    )
    request = request.reshape(devices, cap_slots)
    width = item_embed.shape[1]
    incoming = lax.all_to_all(request, ("grp", "fsdp"), split_axis=0, concat_axis=0, tiled=True)
    found = serve_rows(incoming, item_embed)
    returned = lax.all_to_all(found, ("grp", "fsdp"), split_axis=0, concat_axis=0, tiled=True)
    fetched = jnp.take(returned.reshape(devices * cap_slots, width), position, axis=0)
    hidden = stored(jnp.dot(fetched, adapter, preferred_element_type=jnp.float32))
    user_attention_output, pull = jax.vjp(
        lambda values: user_layer(values, user_gain, query_map), hidden
    )
    (grad_hidden,) = pull(cotangent[0])
    grad_rows = jnp.dot(grad_hidden, adapter.T, preferred_element_type=jnp.float32)
    outgoing = jnp.zeros((devices * cap_slots, DI), jnp.float32).at[position].set(grad_rows)
    arrived = lax.all_to_all(
        outgoing.reshape(devices, cap_slots, DI).astype(jnp.bfloat16),
        ("grp", "fsdp"),
        split_axis=0,
        concat_axis=0,
        tiled=True,
    ).astype(jnp.float32)
    terms = arrived.reshape(devices * cap_slots, DI)
    slot_hot = (
        incoming.reshape(-1)[:, None] == jnp.arange(count, dtype=jnp.int32)[None, :]
    ).astype(jnp.float32)
    item_grad = jnp.dot(slot_hot.T, terms, precision=lax.Precision.HIGHEST)
    return (item_embed, user_attention_output[None], item_grad)


def solution(mesh):
    placed = (
        P(("grp", "fsdp"), None, None),
        P("fsdp", None),
        P("fsdp", None),
        P("fsdp", None),
        P(),
        P("fsdp", None),
        P(),
        P("fsdp", None),
        P(("grp", "fsdp"), None, None),
        P(("grp", "fsdp"), None),
        P(("grp", "fsdp"), None, None),
    )
    return jax.shard_map(
        per_device,
        mesh=mesh,
        in_specs=placed,
        out_specs=(
            P(("grp", "fsdp"), None),
            P(("grp", "fsdp"), None, None),
            P(("grp", "fsdp"), None),
        ),
        check_vma=False,
    )
```

profile of v0, /device:TPU:1, one launch (start us, length us, event | category | flops | bytes accessed | tf_op | source)
XLA Modules:
  0.0 473.3 jit_solution(699172735839082642)
XLA Ops:
  14.3 11.5 %all-to-all-start = ((s32[128,1,2]{2,1,0:T(1,128)}), s32[128,1,2]{2,1,0:T(1,128)S(1)}, u32[]{:S(2)}, u32[]{:S(2)}) async-start(s32[128,1,2]{2,1,0:T(1,128)} %bitcast.7), calls=%async_computation | async-start | bytes 131072 | tf_op jit(solution)/shard_map/all_to_all | solution.py:120
  26.8 8.2 %all-to-all-done = s32[128,1,2]{2,1,0:T(1,128)S(1)} async-done(((s32[128,1,2]{2,1,0:T(1,128)}), s32[128,1,2]{2,1,0:T(1,128)S(1)}, u32[]{:S(2)}, u32[]{:S(2)}) %all-to-all-start) | async-done | bytes 1056 | tf_op jit(solution)/shard_map/all_to_all | solution.py:120
  35.1 41.2 %all-gather.8.cloned.1.call-done = bf16[2048,256]{1,0:T(8,128)(2,1)} async-done(((bf16[32,256]{1,0:T(8,128)(2,1)}), bf16[2048,256]{1,0:T(8,128)(2,1)}) %all-gather.8.cloned.1.call-update) | async-done | bytes 1048592 | tf_op jit(solution)/shard_map/all_gather | solution.py:83
  76.3 3.7 convolution_convert_fusion.7
  80.4 60.2 %all-gather.10.cloned.1.call-done = bf16[2048,256]{1,0:T(8,128)(2,1)} async-done(((bf16[32,256]{1,0:T(8,128)(2,1)}), bf16[2048,256]{1,0:T(8,128)(2,1)}) %all-gather.10.cloned.1.call-update) | async-done | bytes 1048592 | tf_op jit(solution)/shard_map/all_gather | solution.py:88
  140.7 3.7 convolution_convert_fusion.6
  144.8 76.3 %all-gather.6.cloned.1.call-done = bf16[2048,2048]{1,0:T(8,128)(2,1)} async-done(((bf16[32,2048]{1,0:T(8,128)(2,1)}), bf16[2048,2048]{1,0:T(8,128)(2,1)}) %all-gather.6.cloned.1.call-update) | async-done | bytes 8388624 | tf_op jit(solution)/shard_map/all_gather | solution.py:94
  221.1 4.6 convolution_convert_fusion.2
  227.5 2.0 copy.53
  229.5 8.0 %all-to-all-start.1 = ((bf16[128,2,2048]{2,1,0:T(2,128)(2,1)}), bf16[128,2,2048]{2,1,0:T(2,128)(2,1)S(1)}, u32[]{:S(2)}, u32[]{:S(2)}) async-start(bf16[128,2,2048]{2,1,0:T(2,128)(2,1)} %copy.53), calls=%async_computation.1 | async-start | bytes 2097152 | tf_op jit(solution)/shard_map/all_to_all | solution.py:122
  238.9 17.7 %all-to-all-done.1 = bf16[128,2,2048]{2,1,0:T(2,128)(2,1)S(1)} async-done(((bf16[128,2,2048]{2,1,0:T(2,128)(2,1)}), bf16[128,2,2048]{2,1,0:T(2,128)(2,1)S(1)}, u32[]{:S(2)}, u32[]{:S(2)}) %all-to-all-start.1) | async-done | bytes 1048608 | tf_op jit(solution)/shard_map/all_to_all | solution.py:122
  258.0 78.2 %all-gather.12.cloned.1.call-done = bf16[2048,4096]{1,0:T(8,128)(2,1)} async-done(((bf16[32,4096]{1,0:T(8,128)(2,1)}), bf16[2048,4096]{1,0:T(8,128)(2,1)}) %all-gather.12.cloned.1.call-update) | async-done | bytes 16777232 | tf_op jit(solution)/shard_map/all_gather | solution.py:98
  336.2 8.2 %convolution_convert_fusion = bf16[128,4096]{1,0:T(8,128)(2,1)S(1)} fusion(bf16[2048,4096]{1,0:T(8,128)(2,1)} %all-gather.12.cloned.1.call-done, bf16[128,2048]{1,0:T(8,128)(2,1)S(1)} %gather_fusion, pred[128]{0:T(512)(128)(4,1)S(1)} %compare_and_fusion), kind=kOutput, calls=%fused_computation.5 | convolution fusion | flops 2148270080 | bytes 18350208 | tf_op jit(solution)/shard_map/dot_general | solution.py:124
  345.0 55.9 %all-gather.14.cloned.1.call-done = bf16[4096,128]{1,0:T(8,128)(2,1)} async-done(((bf16[64,128]{1,0:T(8,128)(2,1)}), bf16[4096,128]{1,0:T(8,128)(2,1)}) %all-gather.14.cloned.1.call-update) | async-done | bytes 1048592 | tf_op jit(solution)/shard_map/all_gather | solution.py:99
  400.9 2.6 fusion.15
  404.9 3.5 fusion.76
  408.5 2.6 fusion.7
  414.1 1.9 fusion.29
  417.4 2.9 copy.78
  420.3 3.1 fusion.13
  423.4 12.5 %fusion.22 = f32[128,2048]{1,0:T(8,128)} fusion(bf16[2048,4096]{1,0:T(8,128)(2,1)} %all-gather.12.cloned.1.call-done, bf16[128,4096]{1,0:T(8,128)(2,1)S(1)} %convolution_convert_fusion, bf16[128,4096]{1,0:T(8,128)(2,1)S(1)} %copy.80, bf16[1,128,4096]{2,1,0:T(8,128)(2,1)S(1)} %copy-done.2, f32[128]{0:T(128)S(1)} %multiply_multiply_fusion, ...), kind=kOutput, calls=%fused_computation.47 | convolution fusion | flops 2152202240 | bytes 20988928 | tf_op jit(solution)/shard_map/dot_general | solution.py:129
  435.9 2.4 scatter_custom_fusion.1
  440.0 7.6 %all-to-all-start.2 = ((bf16[128,2,2048]{2,1,0:T(2,128)(2,1)}), bf16[128,2,2048]{2,1,0:T(2,128)(2,1)S(1)}, u32[]{:S(2)}, u32[]{:S(2)}) async-start(bf16[128,2,2048]{2,1,0:T(2,128)(2,1)} %convert_element_type.130), calls=%async_computation.2 | async-start | bytes 2097152 | tf_op jit(solution)/shard_map/all_to_all | solution.py:131
  449.0 16.4 %all-to-all-done.2 = bf16[128,2,2048]{2,1,0:T(2,128)(2,1)S(1)} async-done(((bf16[128,2,2048]{2,1,0:T(2,128)(2,1)}), bf16[128,2,2048]{2,1,0:T(2,128)(2,1)S(1)}, u32[]{:S(2)}, u32[]{:S(2)}) %all-to-all-start.2) | async-done | bytes 1048608 | tf_op jit(solution)/shard_map/all_to_all | solution.py:131
  (75 shorter events, 24.3 us)
Async XLA Ops:
  7.2 69.1 %all-gather.8.cloned.1.call-start = ((), (), s32[]{:S(2)}) async-start(), calls=%async_computation.4 | async-start | bytes 1064960 | tf_op jit(solution)/shard_map/all_gather | solution.py:83
  7.9 132.8 %all-gather.10.cloned.1.call-start = ((), (), s32[]{:S(2)}) async-start(), calls=%async_computation.5 | async-start | bytes 1064960 | tf_op jit(solution)/shard_map/all_gather | solution.py:88
  8.6 212.4 %all-gather.6.cloned.1.call-start = ((), (), s32[]{:S(2)}) async-start(), calls=%async_computation.3 | async-start | bytes 8519680 | tf_op jit(solution)/shard_map/all_gather | solution.py:94
  9.4 326.8 %all-gather.12.cloned.1.call-start = ((), (), s32[]{:S(2)}) async-start(), calls=%async_computation.6 | async-start | bytes 17039360 | tf_op jit(solution)/shard_map/all_gather | solution.py:98
  14.3 20.8 %all-to-all-start = ((s32[128,1,2]{2,1,0:T(1,128)}), s32[128,1,2]{2,1,0:T(1,128)S(1)}, u32[]{:S(2)}, u32[]{:S(2)}) async-start(s32[128,1,2]{2,1,0:T(1,128)} %bitcast.7), calls=%async_computation | async-start | bytes 131072 | tf_op jit(solution)/shard_map/all_to_all | solution.py:120
  225.7 1.2 copy-start.8
  227.0 2.6 copy-start.7
  227.5 10.7 %copy-start.1 = (bf16[1,128,4096]{2,1,0:T(8,128)(2,1)S(1)}, bf16[1,128,4096]{2,1,0:T(8,128)(2,1)}, u32[]{:S(2)}) copy-start(bf16[1,128,4096]{2,1,0:T(8,128)(2,1)} %param.21) | copy-start | bytes 3145732
  229.5 9.3 %copy-start.9 = (s32[1,128,1]{1,2,0:T(1,128)S(1)}, s32[1,128,1]{1,2,0:T(1,128)}, u32[]{:S(2)}) copy-start(s32[1,128,1]{1,2,0:T(1,128)} %param.19) | copy-start | bytes 1540
  229.5 27.1 %all-to-all-start.1 = ((bf16[128,2,2048]{2,1,0:T(2,128)(2,1)}), bf16[128,2,2048]{2,1,0:T(2,128)(2,1)S(1)}, u32[]{:S(2)}, u32[]{:S(2)}) async-start(bf16[128,2,2048]{2,1,0:T(2,128)(2,1)} %copy.53), calls=%async_computation.1 | async-start | bytes 2097152 | tf_op jit(solution)/shard_map/all_to_all | solution.py:122
  237.6 163.3 %all-gather.14.cloned.1.call-start = ((), (), s32[]{:S(2)}) async-start(), calls=%async_computation.7 | async-start | bytes 1064960 | tf_op jit(solution)/shard_map/all_gather | solution.py:99
  258.0 86.7 %copy-start.6 = (f32[4096]{0:T(1024)S(1)}, f32[4096]{0:T(1024)}, u32[]{:S(2)}) copy-start(f32[4096]{0:T(1024)} %param.17) | copy-start | bytes 49156
  408.5 2.6 copy-start.3
  408.5 2.9 copy-start.4
  408.5 3.1 copy-start.5
  414.1 1.9 copy-start
  420.3 3.1 copy-start.2
  440.0 25.4 %all-to-all-start.2 = ((bf16[128,2,2048]{2,1,0:T(2,128)(2,1)}), bf16[128,2,2048]{2,1,0:T(2,128)(2,1)S(1)}, u32[]{:S(2)}, u32[]{:S(2)}) async-start(bf16[128,2,2048]{2,1,0:T(2,128)(2,1)} %convert_element_type.130), calls=%async_computation.2 | async-start | bytes 2097152 | tf_op jit(solution)/shard_map/all_to_all | solution.py:131
Sparse Core Ops, SparseCore 0:
  10.9 65.3 all-gather.7
  79.2 61.4 all-gather.9
  143.6 77.4 all-gather.5
  223.8 112.3 all-gather.11
  339.0 61.9 all-gather.13
where the time goes:
time: 474 us; the launch traced here: 473 us
  waiting for transfers between devices  357 us (75%)
  matrix products  47.8 us (10%)
  starting transfers between devices  27.4 us (6%)
  local copies, waits for them, and re-layouts  17 us (4%)
  between operations  14.1 us (3%)
  other arithmetic  9.93 us (2%)
    all_gather x1, waiting for transfers between devices, per_device(): lax.all_gather(w_adapt, 'fsdp', axis=0, tiled=True)  78.2 us
    all_gather x1, waiting for transfers between devices, per_device(): lax.all_gather(w_query, 'fsdp', axis=0, tiled=True)  76.3 us
    all_gather x1, waiting for transfers between devices, per_device(): lax.all_gather(w_value, 'fsdp', axis=0, tiled=True)  60.2 us
    all_gather x1, waiting for transfers between devices, per_device(): lax.all_gather(user_query, 'fsdp', axis=0, tiled=True)  55.9 us
    all_gather x1, waiting for transfers between devices, per_device(): lax.all_gather(w_key, 'fsdp', axis=0, tiled=True)  41.2 us
    all_to_all x1, waiting for transfers between devices, per_device(): lax.all_to_all(found, ('grp', 'fsdp'), split_axis=0, concat_axis=0, tiled...  17.7 us
    all_to_all x1, waiting for transfers between devices, per_device(): lax.all_to_all(outgoing.reshape(devices, cap_slots, DI).astype(jnp.bfloat...  16.4 us
    dot_general x1, matrix products, per_device(): jnp.dot(grad_hidden, adapter.T, preferred_element_type=jnp.float32)  12.5 us
  transfers between devices with their start and end apart: 8, of which 8 were waited for; matrix products, arithmetic and copies ran while one was open for 7% of the time, Pallas kernels for 0%

commit v1 on v0

--- a/solution.py
+++ b/solution.py
@@ -89,10 +89,21 @@
         preferred_element_type=jnp.float32,
     )
     columns = last_row
+
+    def launch_the_lanes(local_x, a_name):
+        top = jnp.concatenate(
+            jax.lax.all_to_all(
+                jnp.stack([local_x] * jax.lax.axis_size(a_name), axis=0),
+                axis_name=a_name,
+                split_axis=0,
+                concat_axis=0,
+            ),
+            axis=0,
+        )
+        return top
+
     query_sum = jnp.dot(
-        columns,
-        lax.all_gather(w_query, "fsdp", axis=0, tiled=True),
-        preferred_element_type=jnp.float32,
+        columns, launch_the_lanes(w_query, "fsdp"), preferred_element_type=jnp.float32
     )
     adapter, query_map = (
         lax.all_gather(w_adapt, "fsdp", axis=0, tiled=True),

time: 474 us -> 492 us (1.038)
  blocking collectives: 0 us -> 20.7 us
  starting transfers between devices: 27.4 us -> 21.2 us
    all_gather x1, waiting for transfers between devices: 41.2 us -> 124 us  [per_device(): lax.all_gather(w_key, 'fsdp', axis=0, tiled=True)]
    all_gather x1 -> x0, waiting for transfers between devices: 76.3 us -> none  [per_device(): lax.all_gather(w_query, 'fsdp', axis=0, tiled=True)]
    all_to_all x0 -> x1, blocking collectives: none -> 20.7 us  [per_device(): lax.all_to_all(request, ('grp', 'fsdp'), split_axis=0, concat_axis=0, til...]
    all_to_all x1, waiting for transfers between devices: 8.22 us -> 0.01 us  [launch_the_lanes(): jax.lax.all_to_all(jnp.stack([local_x] * jax.lax.axis_size(a_name), axis=...]
    all_to_all x1, starting transfers between devices: 11.5 us -> 5.75 us  [launch_the_lanes(): jax.lax.all_to_all(jnp.stack([local_x] * jax.lax.axis_size(a_name), axis=...]
    another operation x0 -> x1, local copies, waits for them, and re-layouts: none -> 5.17 us  [launch_the_lanes(): jnp.stack([local_x] * jax.lax.axis_size(a_name), axis=0)]
  transfers between devices with their start and end apart: 8 -> 7, of which waited for: 8 -> 6; matrix products, arithmetic and copies ran while one was open for 7% -> 8% of each run, Pallas kernels for 0% -> 0%
where the time goes in v1:
time: 492 us; the launch traced here: 491 us
  waiting for transfers between devices  356 us (72%)
  matrix products  47.8 us (10%)
  local copies, waits for them, and re-layouts  21.5 us (4%)
  starting transfers between devices  21.2 us (4%)
  blocking collectives  20.7 us (4%)
  between operations  14.1 us (3%)
  other arithmetic  9.93 us (2%)
    all_gather x1, waiting for transfers between devices, per_device(): lax.all_gather(w_key, 'fsdp', axis=0, tiled=True)  124 us
    all_gather x1, waiting for transfers between devices, per_device(): lax.all_gather(w_adapt, 'fsdp', axis=0, tiled=True)  76.6 us
    all_gather x1, waiting for transfers between devices, per_device(): lax.all_gather(w_value, 'fsdp', axis=0, tiled=True)  63.9 us
    all_gather x1, waiting for transfers between devices, per_device(): lax.all_gather(user_query, 'fsdp', axis=0, tiled=True)  55.9 us
    all_to_all x1, blocking collectives, per_device(): lax.all_to_all(request, ('grp', 'fsdp'), split_axis=0, concat_axis=0, til...  20.7 us
    all_to_all x1, waiting for transfers between devices, per_device(): lax.all_to_all(found, ('grp', 'fsdp'), split_axis=0, concat_axis=0, tiled...  16.8 us
    all_to_all x1, waiting for transfers between devices, per_device(): lax.all_to_all(outgoing.reshape(devices, cap_slots, DI).astype(jnp.bfloat...  16.4 us
    dot_general x1, matrix products, per_device(): jnp.dot(grad_hidden, adapter.T, preferred_element_type=jnp.float32)  12.5 us
  transfers between devices with their start and end apart: 7, of which 6 were waited for; matrix products, arithmetic and copies ran while one was open for 8% of the time, Pallas kernels for 0%

profile of v1, /device:TPU:1, one launch (start us, length us, event | category | flops | bytes accessed | tf_op | source)
XLA Modules:
  0.0 490.9 jit_solution(1776051180005693340)
XLA Ops:
  13.1 20.7 %all_to_all.24 = s32[128,1,2]{2,1,0:T(1,128)S(1)} all-to-all(s32[128,1,2]{2,1,0:T(1,128)S(1)} %bitcast.113), channel_id=1, replica_groups=mesh['grp'=2,'fsdp'=64] {'grp','fsdp'}, dimensions={0} | all-to-all | bytes 2048 | tf_op jit(solution)/shard_map/all_to_all | solution.py:131
  33.7 5.2 %stack.2 = bf16[64,32,2048]{2,1,0:T(8,128)(2,1)} broadcast(bf16[32,2048]{1,0:T(8,128)(2,1)} %param.12), dimensions={1,2} | broadcast | bytes 8519680 | tf_op jit(solution)/shard_map/stack | solution.py:96
  38.9 5.7 %all-to-all-start = ((bf16[64,32,2048]{2,1,0:T(8,128)(2,1)}), bf16[64,32,2048]{2,1,0:T(8,128)(2,1)}, u32[]{:S(2)}, u32[]{:S(2)}) async-start(bf16[64,32,2048]{2,1,0:T(8,128)(2,1)} %stack.2), calls=%async_computation | async-start | bytes 16777216 | tf_op jit(solution)/shard_map/all_to_all | solution.py:95
  45.8 123.5 %all-gather.5.cloned.1.call-done = bf16[2048,256]{1,0:T(8,128)(2,1)} async-done(((bf16[32,256]{1,0:T(8,128)(2,1)}), bf16[2048,256]{1,0:T(8,128)(2,1)}) %all-gather.5.cloned.1.call-update) | async-done | bytes 1048592 | tf_op jit(solution)/shard_map/all_gather | solution.py:83
  169.3 3.7 convolution_convert_fusion.7
  173.5 63.9 %all-gather.7.cloned.1.call-done = bf16[2048,256]{1,0:T(8,128)(2,1)} async-done(((bf16[32,256]{1,0:T(8,128)(2,1)}), bf16[2048,256]{1,0:T(8,128)(2,1)}) %all-gather.7.cloned.1.call-update) | async-done | bytes 1048592 | tf_op jit(solution)/shard_map/all_gather | solution.py:88
  237.4 3.7 convolution_convert_fusion.6
  241.6 4.6 convolution_convert_fusion.2
  248.0 2.0 copy.53
  250.0 7.6 %all-to-all-start.2 = ((bf16[128,2,2048]{2,1,0:T(2,128)(2,1)}), bf16[128,2,2048]{2,1,0:T(2,128)(2,1)S(1)}, u32[]{:S(2)}, u32[]{:S(2)}) async-start(bf16[128,2,2048]{2,1,0:T(2,128)(2,1)} %copy.53), calls=%async_computation.2 | async-start | bytes 2097152 | tf_op jit(solution)/shard_map/all_to_all | solution.py:133
  258.9 16.8 %all-to-all-done.2 = bf16[128,2,2048]{2,1,0:T(2,128)(2,1)S(1)} async-done(((bf16[128,2,2048]{2,1,0:T(2,128)(2,1)}), bf16[128,2,2048]{2,1,0:T(2,128)(2,1)S(1)}, u32[]{:S(2)}, u32[]{:S(2)}) %all-to-all-start.2) | async-done | bytes 1048608 | tf_op jit(solution)/shard_map/all_to_all | solution.py:133
  277.1 76.6 %all-gather.9.cloned.1.call-done = bf16[2048,4096]{1,0:T(8,128)(2,1)} async-done(((bf16[32,4096]{1,0:T(8,128)(2,1)}), bf16[2048,4096]{1,0:T(8,128)(2,1)}) %all-gather.9.cloned.1.call-update) | async-done | bytes 16777232 | tf_op jit(solution)/shard_map/all_gather | solution.py:109
  353.8 8.2 %convolution_convert_fusion = bf16[128,4096]{1,0:T(8,128)(2,1)S(1)} fusion(bf16[2048,4096]{1,0:T(8,128)(2,1)} %all-gather.9.cloned.1.call-done, bf16[128,2048]{1,0:T(8,128)(2,1)S(1)} %gather_fusion, pred[128]{0:T(512)(128)(4,1)S(1)} %compare_and_fusion), kind=kOutput, calls=%fused_computation.5 | convolution fusion | flops 2148270080 | bytes 18350208 | tf_op jit(solution)/shard_map/dot_general | solution.py:135
  362.6 55.9 %all-gather.11.cloned.1.call-done = bf16[4096,128]{1,0:T(8,128)(2,1)} async-done(((bf16[64,128]{1,0:T(8,128)(2,1)}), bf16[4096,128]{1,0:T(8,128)(2,1)}) %all-gather.11.cloned.1.call-update) | async-done | bytes 1048592 | tf_op jit(solution)/shard_map/all_gather | solution.py:110
  418.5 2.6 fusion.15
  422.5 3.5 fusion.76
  426.0 2.6 fusion.7
  431.6 1.9 fusion.29
  434.9 2.9 copy.78
  437.8 3.1 fusion.13
  441.0 12.5 %fusion.22 = f32[128,2048]{1,0:T(8,128)} fusion(bf16[2048,4096]{1,0:T(8,128)(2,1)} %all-gather.9.cloned.1.call-done, bf16[128,4096]{1,0:T(8,128)(2,1)S(1)} %convolution_convert_fusion, bf16[128,4096]{1,0:T(8,128)(2,1)S(1)} %copy.80, bf16[1,128,4096]{2,1,0:T(8,128)(2,1)S(1)} %copy-done.2, f32[128]{0:T(128)S(1)} %multiply_multiply_fusion, ...), kind=kOutput, calls=%fused_computation.47 | convolution fusion | flops 2152202240 | bytes 20988928 | tf_op jit(solution)/shard_map/dot_general | solution.py:140
  453.4 2.4 scatter_custom_fusion.1
  457.5 7.6 %all-to-all-start.3 = ((bf16[128,2,2048]{2,1,0:T(2,128)(2,1)}), bf16[128,2,2048]{2,1,0:T(2,128)(2,1)S(1)}, u32[]{:S(2)}, u32[]{:S(2)}) async-start(bf16[128,2,2048]{2,1,0:T(2,128)(2,1)} %convert_element_type.130), calls=%async_computation.3 | async-start | bytes 2097152 | tf_op jit(solution)/shard_map/all_to_all | solution.py:142
  466.6 16.4 %all-to-all-done.3 = bf16[128,2,2048]{2,1,0:T(2,128)(2,1)S(1)} async-done(((bf16[128,2,2048]{2,1,0:T(2,128)(2,1)}), bf16[128,2,2048]{2,1,0:T(2,128)(2,1)S(1)}, u32[]{:S(2)}, u32[]{:S(2)}) %all-to-all-start.3) | async-done | bytes 1048608 | tf_op jit(solution)/shard_map/all_to_all | solution.py:142
  (74 shorter events, 23.1 us)
Async XLA Ops:
  7.2 162.2 %all-gather.5.cloned.1.call-start = ((), (), s32[]{:S(2)}) async-start(), calls=%async_computation.4 | async-start | bytes 1064960 | tf_op jit(solution)/shard_map/all_gather | solution.py:83
  7.9 229.5 %all-gather.7.cloned.1.call-start = ((), (), s32[]{:S(2)}) async-start(), calls=%async_computation.5 | async-start | bytes 1064960 | tf_op jit(solution)/shard_map/all_gather | solution.py:88
  8.6 345.1 %all-gather.9.cloned.1.call-start = ((), (), s32[]{:S(2)}) async-start(), calls=%async_computation.6 | async-start | bytes 17039360 | tf_op jit(solution)/shard_map/all_gather | solution.py:109
  38.9 202.7 %all-to-all-start = ((bf16[64,32,2048]{2,1,0:T(8,128)(2,1)}), bf16[64,32,2048]{2,1,0:T(8,128)(2,1)}, u32[]{:S(2)}, u32[]{:S(2)}) async-start(bf16[64,32,2048]{2,1,0:T(8,128)(2,1)} %stack.2), calls=%async_computation | async-start | bytes 16777216 | tf_op jit(solution)/shard_map/all_to_all | solution.py:95
  246.1 1.2 copy-start.8
  247.4 2.6 copy-start.7
  248.0 10.2 %copy-start.1 = (bf16[1,128,4096]{2,1,0:T(8,128)(2,1)S(1)}, bf16[1,128,4096]{2,1,0:T(8,128)(2,1)}, u32[]{:S(2)}) copy-start(bf16[1,128,4096]{2,1,0:T(8,128)(2,1)} %param.21) | copy-start | bytes 3145732
  250.0 8.9 %copy-start.9 = (s32[1,128,1]{1,2,0:T(1,128)S(1)}, s32[1,128,1]{1,2,0:T(1,128)}, u32[]{:S(2)}) copy-start(s32[1,128,1]{1,2,0:T(1,128)} %param.19) | copy-start | bytes 1540
  250.0 25.7 %all-to-all-start.2 = ((bf16[128,2,2048]{2,1,0:T(2,128)(2,1)}), bf16[128,2,2048]{2,1,0:T(2,128)(2,1)S(1)}, u32[]{:S(2)}, u32[]{:S(2)}) async-start(bf16[128,2,2048]{2,1,0:T(2,128)(2,1)} %copy.53), calls=%async_computation.2 | async-start | bytes 2097152 | tf_op jit(solution)/shard_map/all_to_all | solution.py:133
  257.6 160.8 %all-gather.11.cloned.1.call-start = ((), (), s32[]{:S(2)}) async-start(), calls=%async_computation.7 | async-start | bytes 1064960 | tf_op jit(solution)/shard_map/all_gather | solution.py:110
  277.1 85.1 %copy-start.6 = (f32[4096]{0:T(1024)S(1)}, f32[4096]{0:T(1024)}, u32[]{:S(2)}) copy-start(f32[4096]{0:T(1024)} %param.17) | copy-start | bytes 49156
  426.0 2.6 copy-start.3
  426.0 2.9 copy-start.4
  426.0 3.1 copy-start.5
  431.6 1.9 copy-start
  437.8 3.1 copy-start.2
  457.5 25.4 %all-to-all-start.3 = ((bf16[128,2,2048]{2,1,0:T(2,128)(2,1)}), bf16[128,2,2048]{2,1,0:T(2,128)(2,1)S(1)}, u32[]{:S(2)}, u32[]{:S(2)}) async-start(bf16[128,2,2048]{2,1,0:T(2,128)(2,1)} %convert_element_type.130), calls=%async_computation.3 | async-start | bytes 2097152 | tf_op jit(solution)/shard_map/all_to_all | solution.py:142
Sparse Core Ops, SparseCore 0:
  10.9 158.4 all-gather.4
  172.2 65.1 all-gather.6
  240.3 113.4 all-gather.8
  356.5 61.9 all-gather.10
